TPU v7x, 32 devices: a whole 2x2x4 slice. The times are simulated.
32 devices in a mesh: groups: 2 (over y), col: 4 (over z), aux: 2 (over x), rep: 2 (over core).
Axes of the slice: x: 2, y: 2, z: 4, core: 2. Of those that a mesh axis runs over, the one named last changes fastest.
Arguments:
- b_aux: bfloat16 [4, 4096, 2400], P(('groups', 'aux'), ('col', 'rep')), parts along dimension 0, may hold values from -0.59765625 to 0.59765625
- occ_energies: float32 [2], P('groups'), parts along dimension 0, may hold values from -2 to -0.3
- vir_energies: float32 [4800], P('groups'), parts along dimension 0, may hold values from 0.2 to 3
- owners: int32 [2], replicated, may hold values from 0 to 7
Outputs:
- gamma: float32 [4, 4096, 2400], P(('groups', 'aux'), None, ('col', 'rep')), parts along dimension 0
There are 2 independent parts, one for each index of `groups`. A program takes and returns all parts, laid end to end along the dimension named above; an argument that names none is the same for every part. Nothing has to cross between parts.
Inputs may be any that keep to these rules, and one draw needn't show every extreme that they name: owners[s] is a column shard index in the order of col+rep; owners may repeat.
All inputs are finite; a program needn't handle non-finite values.
Results may differ from a plain program's by a relative error of at most 0.003.
Values may be sent and summed in bfloat16 or wider, within the bound.
No kernel may reach another device: no remote copies, remote signals or barrier semaphores. Data moves between devices by JAX's collectives and lax.ppermute only.
A program may use at most 64 MiB of HBM per device.

v0:
```python
import jax
import jax.numpy as jnp
from jax import lax
from jax.sharding import PartitionSpec as P

os_scale = 1.3


def from_root(value, axis, source):
    kept = jnp.where(lax.axis_index(axis) == source, value, 0).astype(value.dtype)
    return lax.psum(kept, axis)


def column_energy(first, occ_energies, vir_energies, width):
    nvirt = vir_energies.shape[0]
    occ_value = lax.dynamic_index_in_dim(occ_energies, first // nvirt, 0, keepdims=False)
    vir_values = lax.dynamic_slice_in_dim(vir_energies, first % nvirt, width, 0)
    return vir_values - occ_value


def body(b_aux, occ_energies, vir_energies, owners):
    moved = lax.all_to_all(b_aux, ("col", "rep"), split_axis=2, concat_axis=1, tiled=True)
    local_cols = moved[0]
    width = local_cols.shape[1]
    shard_index = lax.axis_index(("col", "rep"))
    energy_mine = column_energy(shard_index * width, occ_energies, vir_energies, width)
    gamma_acc = jnp.zeros(local_cols.shape, jnp.float32)
    for step_index in range(owners.shape[0]):
        owner_shard = owners[step_index]
        owner_cols = from_root(local_cols, ("col", "rep"), owner_shard)
        owner_energy = column_energy(owner_shard * width, occ_energies, vir_energies, width)
        denominator = energy_mine[:, None] + owner_energy[None, :]
        partial_value = lax.dot_general(
            local_cols, owner_cols, (((0,), (0,)), ((), ())), preferred_element_type=jnp.float32
        )
        coupling = lax.psum(partial_value, "aux")
        amplitude = (os_scale * coupling / denominator).astype(jnp.bfloat16)
        gamma_acc = gamma_acc + lax.dot_general(
            owner_cols, amplitude, (((1,), (1,)), ((), ())), preferred_element_type=jnp.float32
        )
    return gamma_acc[None]


def solution(mesh):
    placed = (P(("groups", "aux"), ("col", "rep"), None), P("groups"), P("groups"), P())
    return jax.shard_map(
        body,
        mesh=mesh,
        in_specs=placed,
        out_specs=P(("groups", "aux"), None, ("col", "rep")),
        check_vma=False,
    )
```

profile of v0, /device:TPU:0, one launch (start us, length us, event | category | flops | bytes accessed | tf_op | source)
XLA Modules:
  0.0 311.1 jit_solution(7487857900732730221)
XLA Ops:
  6.5 13.4 %copy.16 = bf16[1,512,2400]{1,0,2:T(2,128)(2,1)} copy(bf16[1,512,2400]{1,2,0:T(8,128)(2,1)} %param.4) | data formatting | bytes 4915200 | tf_op args[0]
  20.0 0.6 broadcast.16
  20.6 16.3 %reduce.2 = bf16[2400,512]{1,0:T(8,128)(2,1)S(1)} reduce(bf16[2400,1,512]{2,1,0:T(2,128)(2,1)} %bitcast.32, bf16[]{:T(256)} %broadcast.16), dimensions={1}, to_apply=%bitcast.30.reduce_sub_computation | reduce | bytes 4915202
  36.9 2.4 reshape.5
  39.3 6.5 %all-to-all-start = ((bf16[8,2,76800]{2,1,0:T(2,128)(2,1)}), bf16[8,2,76800]{2,1,0:T(2,128)(2,1)S(1)}, u32[]{:S(2)}, u32[]{:S(2)}) async-start(bf16[8,2,76800]{2,1,0:T(2,128)(2,1)} %reshape.5), calls=%async_computation | async-start | bytes 4915200 | tf_op jit(solution)/shard_map/all_to_all | solution.py:22
  45.7 0.0 all-reduce.7.cloned.1.call-start
  45.8 0.6 fusion.10
  47.7 54.8 %all-to-all-done = bf16[8,2,76800]{2,1,0:T(2,128)(2,1)S(1)} async-done(((bf16[8,2,76800]{2,1,0:T(2,128)(2,1)}), bf16[8,2,76800]{2,1,0:T(2,128)(2,1)S(1)}, u32[]{:S(2)}, u32[]{:S(2)}) %all-to-all-start) | async-done | bytes 2457632 | tf_op jit(solution)/shard_map/all_to_all | solution.py:22
  102.5 4.4 %reshape.6 = bf16[2400,1,512]{2,1,0:T(2,128)(2,1)} reshape(bf16[8,2,76800]{2,1,0:T(2,128)(2,1)S(1)} %all-to-all-done) | data formatting | bytes 4915200
  107.0 17.2 %bitcast_reduce_fusion = bf16[512,2400]{0,1:T(8,128)(2,1)} fusion(bf16[2400,1,512]{2,1,0:T(2,128)(2,1)} %reshape.6), kind=kLoop, calls=%fused_computation.22 | loop fusion | bytes 4915200 | tf_op jit(solution)/shard_map/all_to_all | solution.py:22
  124.1 2.6 all_to_all.12
  126.8 1.4 copy.15
  128.1 0.2 pad
  128.3 1.1 copy.12
  129.4 2.6 broadcast_select_fusion
  132.1 0.2 all-reduce.5.cloned.1.call-start
  132.3 110.6 %all-reduce.7.cloned.1.call-done = (bf16[4096,300]{0,1:T(8,128)(2,1)}, bf16[4096,300]{0,1:T(8,128)(2,1)}) async-done(((bf16[4096,300]{0,1:T(8,128)(2,1)}, bf16[4096,300]{0,1:T(8,128)(2,1)}), (bf16[4096,300]{0,1:T(8,128)(2,1)}, bf16[4096,300]{0,1:T(8,128)(2,1)})) %all-reduce.7.cloned.1.call-update) | async-done | bytes 4915216 | tf_op jit(solution)/shard_map/psum | solution.py:11
  242.9 4.1 %convolution_bitcast_fusion.1 = f32[300,300]{0,1:T(8,128)} fusion(bf16[4096,300]{0,1:T(8,128)(2,1)} %get-tuple-element.7, bf16[4096,300]{0,1:T(8,128)(2,1)S(1)} %bitcast.34), kind=kOutput, calls=%fused_computation.6 | convolution fusion | flops 737280000 | bytes 5275200 | tf_op jit(solution)/shard_map/dot_general | solution.py:33
  247.0 2.3 convolution_bitcast_fusion
  251.2 0.1 dynamic-slice_subtract_fusion
  251.3 35.9 %all-reduce.5.cloned.1.call-done = (f32[300,300]{0,1:T(8,128)}, f32[300,300]{0,1:T(8,128)}) async-done(((f32[300,300]{0,1:T(8,128)}, f32[300,300]{0,1:T(8,128)}), (f32[300,300]{0,1:T(8,128)}, f32[300,300]{0,1:T(8,128)})) %all-reduce.5.cloned.1.call-update) | async-done | bytes 720016 | tf_op jit(solution)/shard_map/psum | solution.py:36
  287.2 3.5 %fusion.1 = f32[4096,300]{0,1:T(8,128)S(1)} fusion(bf16[4096,300]{0,1:T(8,128)(2,1)} %get-tuple-element.7, f32[300,300]{0,1:T(8,128)} %get-tuple-element.5, f32[300]{0:T(512)S(1)} %get-tuple-element.13, f32[300]{0:T(512)S(1)} %get-tuple-element.12), kind=kOutput, calls=%fused_computation.9 | convolution fusion | flops 737640000 | bytes 7735200 | tf_op jit(solution)/shard_map/dot_general | solution.py:38
  290.7 3.9 %fusion = f32[1,4096,300]{1,2,0:T(8,128)} fusion(f32[4096,300]{0,1:T(8,128)S(1)} %fusion.1, bf16[4096,300]{0,1:T(8,128)(2,1)S(1)} %copy-done.1, f32[300,300]{0,1:T(8,128)S(1)} %copy-done.2, f32[300]{0:T(512)S(1)} %get-tuple-element.11, f32[300]{0:T(512)S(1)} %get-tuple-element.12), kind=kOutput, calls=%fused_computation.1 | convolution fusion | flops 738868800 | bytes 12650400 | tf_op jit(solution)/shard_map/dot_general | solution.py:38
  294.6 9.7 %copy.10 = f32[1,4096,300]{1,0,2:T(1,128)} copy(f32[1,4096,300]{1,2,0:T(8,128)} %fusion) | data formatting | bytes 9830400 | tf_op jit(solution)/shard_map/broadcast_in_dim | solution.py:41
  (12 shorter events, 0.1 us)
Async XLA Ops:
  39.3 6.5 %copy-start.4 = (s32[2]{0:T(128)S(1)}, s32[2]{0:T(128)}, u32[]{:S(2)}) copy-start(s32[2]{0:T(128)} %param.7) | copy-start | bytes 28
  39.3 63.2 %all-to-all-start = ((bf16[8,2,76800]{2,1,0:T(2,128)(2,1)}), bf16[8,2,76800]{2,1,0:T(2,128)(2,1)S(1)}, u32[]{:S(2)}, u32[]{:S(2)}) async-start(bf16[8,2,76800]{2,1,0:T(2,128)(2,1)} %reshape.5), calls=%async_computation | async-start | bytes 4915200 | tf_op jit(solution)/shard_map/all_to_all | solution.py:22
  45.7 197.1 %all-reduce.7.cloned.1.call-start = ((), (), s32[]{:S(2)}) async-start(), calls=%async_computation.2 | async-start | bytes 9961472 | tf_op jit(solution)/shard_map/psum | solution.py:11
  132.1 155.1 %all-reduce.5.cloned.1.call-start = ((), (), s32[]{:S(2)}) async-start(), calls=%async_computation.1 | async-start | bytes 1867776 | tf_op jit(solution)/shard_map/psum | solution.py:36
  242.9 4.1 %copy-start = (bf16[4096,300]{0,1:T(8,128)(2,1)S(1)}, bf16[4096,300]{0,1:T(8,128)(2,1)}, u32[]{:S(2)}) copy-start(bf16[4096,300]{0,1:T(8,128)(2,1)} %get-tuple-element.8) | copy-start | bytes 7372804
  247.0 4.2 %copy-start.3 = (f32[2400]{0:T(1024)S(1)}, f32[2400]{0:T(1024)}, u32[]{:S(2)}) copy-start(f32[2400]{0:T(1024)} %param.6) | copy-start | bytes 28804
  287.2 3.5 %copy-start.1 = (bf16[4096,300]{0,1:T(8,128)(2,1)S(1)}, bf16[4096,300]{0,1:T(8,128)(2,1)}, u32[]{:S(2)}) copy-start(bf16[4096,300]{0,1:T(8,128)(2,1)} %get-tuple-element.8) | copy-start | bytes 7372804
  287.2 3.5 %copy-start.2 = (f32[300,300]{0,1:T(8,128)S(1)}, f32[300,300]{0,1:T(8,128)}, u32[]{:S(2)}) copy-start(f32[300,300]{0,1:T(8,128)} %get-tuple-element.6) | copy-start | bytes 1080004
Sparse Core Ops, SparseCore 0:
  132.2 110.6 all-reduce.6
  249.4 37.7 all-reduce.4
where the time goes:
time: 312 us; the launch traced here: 311 us
  waiting for transfers between devices  201 us (64%)
  local copies, waits for them, and re-layouts  53.6 us (17%)
  other arithmetic  19.1 us (6%)
  between operations  16.7 us (5%)
  matrix products  13.7 us (4%)
  starting transfers between devices  6.72 us (2%)
    psum x1, waiting for transfers between devices, from_root(): return lax.psum(kept, axis)  111 us
    all_to_all x1, waiting for transfers between devices, body(): lax.all_to_all(b_aux, ('col', 'rep'), split_axis=2, concat_axis=1, tiled=...  54.8 us
    psum x1, waiting for transfers between devices, body(): coupling = lax.psum(partial_value, 'aux')  35.9 us
    unnamed x16, local copies, waits for them, and re-layouts  22.1 us
    all_to_all x3, local copies, waits for them, and re-layouts, body(): lax.all_to_all(b_aux, ('col', 'rep'), split_axis=2, concat_axis=1, tiled=...  21.1 us
    unnamed x1, other arithmetic  16.3 us
    broadcast_in_dim x1, local copies, waits for them, and re-layouts, body(): return gamma_acc[None]  9.71 us
    dot_general x2, matrix products, body(): lax.dot_general(owner_cols, amplitude, (((1,), (1,)), ((), ())), preferre...  7.4 us
  transfers between devices with their start and end apart: 3, of which 3 were waited for; matrix products, arithmetic and copies ran while one was open for 0% of the time, Pallas kernels for 0%

commit v1 on v0

--- a/solution.py
+++ b/solution.py
@@ -19,7 +19,12 @@
 
 
 def body(b_aux, occ_energies, vir_energies, owners):
-    moved = lax.all_to_all(b_aux, ("col", "rep"), split_axis=2, concat_axis=1, tiled=True)
+    moved = jnp.concatenate(
+        lax.all_to_all(
+            jnp.stack(jnp.split(b_aux, lax.axis_size(("col", "rep")), axis=2)), ("col", "rep"), 0, 0
+        ),
+        axis=1,
+    )
     local_cols = moved[0]
     width = local_cols.shape[1]
     shard_index = lax.axis_index(("col", "rep"))

time: 312 us -> 265 us (0.85)
  local copies, waits for them, and re-layouts: 53.6 us -> 23.2 us
  other arithmetic: 19.1 us -> 2.72 us
    all_to_all x3 -> x1, local copies, waits for them, and re-layouts: 21.1 us -> 1.36 us  [body(): lax.all_to_all(jnp.stack(jnp.split(b_aux, lax.axis_size(('col', 'rep')),...]
    unnamed x1 -> x0, other arithmetic: 16.3 us -> none
    unnamed x16 -> x21, local copies, waits for them, and re-layouts: 22.1 us -> 10.7 us
where the time goes in v1:
time: 265 us
  waiting for transfers between devices  202 us (76%)
  local copies, waits for them, and re-layouts  23.2 us (9%)
  between operations  16.8 us (6%)
  matrix products  13.6 us (5%)
  starting transfers between devices  6.72 us (3%)
  other arithmetic  2.72 us (1%)
    psum x1, waiting for transfers between devices, from_root(): return lax.psum(kept, axis)  111 us
    all_to_all x1, waiting for transfers between devices, body(): lax.all_to_all(jnp.stack(jnp.split(b_aux, lax.axis_size(('col', 'rep')),...  55.5 us
    psum x1, waiting for transfers between devices, body(): coupling = lax.psum(partial_value, 'aux')  35.8 us
    unnamed x21, local copies, waits for them, and re-layouts  10.7 us
    broadcast_in_dim x1, local copies, waits for them, and re-layouts, body(): return gamma_acc[None]  9.71 us
    dot_general x2, matrix products, body(): lax.dot_general(owner_cols, amplitude, (((1,), (1,)), ((), ())), preferre...  7.25 us
    all_to_all x1, starting transfers between devices, body(): lax.all_to_all(jnp.stack(jnp.split(b_aux, lax.axis_size(('col', 'rep')),...  6.46 us
    dot_general x2, matrix products, body(): lax.dot_general(local_cols, owner_cols, (((0,), (0,)), ((), ())), preferr...  6.35 us
  transfers between devices with their start and end apart: 3, of which 3 were waited for; matrix products, arithmetic and copies ran while one was open for 0% of the time, Pallas kernels for 0%

profile of v1, /device:TPU:0, one launch (start us, length us, event | category | flops | bytes accessed | tf_op | source)
XLA Modules:
  0.0 264.9 jit_solution(1040734693330471594)
XLA Ops:
  6.5 1.9 bitcast_dynamic-update-slice_fusion.7
  8.4 1.8 bitcast_dynamic-update-slice_fusion.6
  10.2 1.7 bitcast_dynamic-update-slice_fusion.5
  11.9 1.8 bitcast_dynamic-update-slice_fusion.4
  13.6 0.7 bitcast_dynamic-update-slice_fusion.3
  14.4 0.8 bitcast_dynamic-update-slice_fusion.2
  15.2 0.7 bitcast_dynamic-update-slice_fusion.1
  15.9 0.8 bitcast_dynamic-update-slice_fusion
  16.7 6.5 %all-to-all-start = ((bf16[8,1,512,300]{2,3,1,0:T(8,128)(2,1)}), bf16[8,1,512,300]{2,3,1,0:T(8,128)(2,1)S(1)}, u32[]{:S(2)}, u32[]{:S(2)}) async-start(bf16[8,1,512,300]{2,3,1,0:T(8,128)(2,1)} %bitcast_dynamic-update-slice_fusion), calls=%async_computation | async-start | bytes 4980736 | tf_op jit(solution)/shard_map/all_to_all | solution.py:23
  23.2 0.7 fusion.10
  25.2 55.5 %all-to-all-done = bf16[8,1,512,300]{2,3,1,0:T(8,128)(2,1)S(1)} async-done(((bf16[8,1,512,300]{2,3,1,0:T(8,128)(2,1)}), bf16[8,1,512,300]{2,3,1,0:T(8,128)(2,1)S(1)}, u32[]{:S(2)}, u32[]{:S(2)}) %all-to-all-start) | async-done | bytes 2457632 | tf_op jit(solution)/shard_map/all_to_all | solution.py:23
  80.6 1.4 copy.10
  82.0 0.2 pad
  82.2 1.1 copy.8
  83.3 2.6 broadcast_select_fusion
  86.0 0.2 all-reduce.5.cloned.1.call-start
  86.2 110.6 %all-reduce.7.cloned.1.call-done = (bf16[4096,300]{0,1:T(8,128)(2,1)}, bf16[4096,300]{0,1:T(8,128)(2,1)}) async-done(((bf16[4096,300]{0,1:T(8,128)(2,1)}, bf16[4096,300]{0,1:T(8,128)(2,1)}), (bf16[4096,300]{0,1:T(8,128)(2,1)}, bf16[4096,300]{0,1:T(8,128)(2,1)})) %all-reduce.7.cloned.1.call-update) | async-done | bytes 4915216 | tf_op jit(solution)/shard_map/psum | solution.py:11
  196.8 4.1 %fusion.11 = f32[300,300]{1,0:T(8,128)} fusion(bf16[4096,300]{0,1:T(8,128)(2,1)S(1)} %bitcast.37, bf16[4096,300]{0,1:T(8,128)(2,1)} %get-tuple-element.7), kind=kOutput, calls=%fused_computation.28 | convolution fusion | flops 737280000 | bytes 5275200 | tf_op jit(solution)/shard_map/dot_general | solution.py:38
  200.8 2.3 fusion.12
  205.1 0.1 dynamic-slice_subtract_fusion
  205.2 35.8 %all-reduce.5.cloned.1.call-done = (f32[300,300]{1,0:T(8,128)}, f32[300,300]{1,0:T(8,128)}) async-done(((f32[300,300]{1,0:T(8,128)}, f32[300,300]{1,0:T(8,128)}), (f32[300,300]{1,0:T(8,128)}, f32[300,300]{1,0:T(8,128)})) %all-reduce.5.cloned.1.call-update) | async-done | bytes 720016 | tf_op jit(solution)/shard_map/psum | solution.py:41
  241.1 3.4 %fusion.1 = f32[4096,300]{0,1:T(8,128)S(1)} fusion(bf16[4096,300]{0,1:T(8,128)(2,1)} %get-tuple-element.7, f32[300,300]{1,0:T(8,128)} %get-tuple-element.5, f32[300]{0:T(512)S(1)} %get-tuple-element.13, f32[300]{0:T(512)S(1)} %get-tuple-element.12), kind=kOutput, calls=%fused_computation.15 | convolution fusion | flops 737640000 | bytes 7735200 | tf_op jit(solution)/shard_map/dot_general | solution.py:43
  244.5 3.8 %fusion = f32[1,4096,300]{1,2,0:T(8,128)} fusion(f32[4096,300]{0,1:T(8,128)S(1)} %fusion.1, bf16[4096,300]{0,1:T(8,128)(2,1)S(1)} %copy-done.1, f32[300,300]{1,0:T(8,128)S(1)} %copy-done.3, f32[300]{0:T(512)S(1)} %get-tuple-element.11, f32[300]{0:T(512)S(1)} %get-tuple-element.12), kind=kOutput, calls=%fused_computation.1 | convolution fusion | flops 738868800 | bytes 12650400 | tf_op jit(solution)/shard_map/dot_general | solution.py:43
  248.3 9.7 %copy.7 = f32[1,4096,300]{1,0,2:T(1,128)} copy(f32[1,4096,300]{1,2,0:T(8,128)} %fusion) | data formatting | bytes 9830400 | tf_op jit(solution)/shard_map/broadcast_in_dim | solution.py:46
  (15 shorter events, 0.1 us)
Async XLA Ops:
  6.5 7.1 %copy-start.2 = (bf16[1,512,2400]{1,2,0:T(8,128)(2,1)S(1)}, bf16[1,512,2400]{1,2,0:T(8,128)(2,1)}, u32[]{:S(2)}) copy-start(bf16[1,512,2400]{1,2,0:T(8,128)(2,1)} %param.4) | copy-start | bytes 7372804
  16.7 6.5 %copy-start.5 = (s32[2]{0:T(128)S(1)}, s32[2]{0:T(128)}, u32[]{:S(2)}) copy-start(s32[2]{0:T(128)} %param.7) | copy-start | bytes 28
  16.7 64.0 %all-to-all-start = ((bf16[8,1,512,300]{2,3,1,0:T(8,128)(2,1)}), bf16[8,1,512,300]{2,3,1,0:T(8,128)(2,1)S(1)}, u32[]{:S(2)}, u32[]{:S(2)}) async-start(bf16[8,1,512,300]{2,3,1,0:T(8,128)(2,1)} %bitcast_dynamic-update-slice_fusion), calls=%async_computation | async-start | bytes 4980736 | tf_op jit(solution)/shard_map/all_to_all | solution.py:23
  23.1 173.6 %all-reduce.7.cloned.1.call-start = ((), (), s32[]{:S(2)}) async-start(), calls=%async_computation.2 | async-start | bytes 9961472 | tf_op jit(solution)/shard_map/psum | solution.py:11
  86.0 155.1 %all-reduce.5.cloned.1.call-start = ((), (), s32[]{:S(2)}) async-start(), calls=%async_computation.1 | async-start | bytes 1867776 | tf_op jit(solution)/shard_map/psum | solution.py:41
  196.8 4.1 %copy-start = (bf16[4096,300]{0,1:T(8,128)(2,1)S(1)}, bf16[4096,300]{0,1:T(8,128)(2,1)}, u32[]{:S(2)}) copy-start(bf16[4096,300]{0,1:T(8,128)(2,1)} %get-tuple-element.8) | copy-start | bytes 7372804
  200.8 4.3 %copy-start.4 = (f32[2400]{0:T(1024)S(1)}, f32[2400]{0:T(1024)}, u32[]{:S(2)}) copy-start(f32[2400]{0:T(1024)} %param.6) | copy-start | bytes 28804
  241.1 3.4 %copy-start.1 = (bf16[4096,300]{0,1:T(8,128)(2,1)S(1)}, bf16[4096,300]{0,1:T(8,128)(2,1)}, u32[]{:S(2)}) copy-start(bf16[4096,300]{0,1:T(8,128)(2,1)} %get-tuple-element.8) | copy-start | bytes 7372804
  241.1 3.4 %copy-start.3 = (f32[300,300]{1,0:T(8,128)S(1)}, f32[300,300]{1,0:T(8,128)}, u32[]{:S(2)}) copy-start(f32[300,300]{1,0:T(8,128)} %get-tuple-element.6) | copy-start | bytes 1080004
Sparse Core Ops, SparseCore 0:
  86.1 110.6 all-reduce.6
  203.3 37.7 all-reduce.4
